TPU v7x, 128 devices: a whole 4x4x4 slice. The times are simulated.
128 devices in a mesh: seq: 32 (over x, y, core), wa: 4 (over z).
Axes of the slice: x: 4, y: 4, z: 4, core: 2. Of those that a mesh axis runs over, the one named last changes fastest.
Arguments:
- hidden_in: bfloat16 [16384, 2048], P('seq', 'wa'), may hold values from -6 to 6
- request_spans: int32 [4, 2], replicated, may hold values from 0 to 16384, as said below
- owners: int32 [4], replicated, may hold values from 0 to 31, as said below
- mixer_gain: float32 [2048], replicated, may hold values from 0.1 to 1.9
- query_weight: bfloat16 [2048, 2048], P(None, 'wa'), may hold values from -0.125 to 0.125
- forget_weight: bfloat16 [2048, 2048], P(None, 'wa'), may hold values from -0.0625 to 0.0625
- input_weight: bfloat16 [2048, 2048], P(None, 'wa'), may hold values from -0.125 to 0.125
- gate_weight: bfloat16 [2048, 2048], P(None, 'wa'), may hold values from -0.125 to 0.125
- forget_bias: float32 [2048], P('wa')
- output_weight: bfloat16 [2048, 2048], P('wa'), may hold values from -0.125 to 0.125
- swiglu_gain: float32 [2048], replicated, may hold values from 0.1 to 1.9
- swiglu_gate: bfloat16 [2048, 3072], P(None, 'wa'), may hold values from -0.125 to 0.125
- swiglu_up: bfloat16 [2048, 3072], P(None, 'wa'), may hold values from -0.125 to 0.125
- swiglu_down: bfloat16 [3072, 2048], P('wa'), may hold values from -0.109375 to 0.109375
Outputs:
- hidden_out: bfloat16 [16384, 2048], P('seq', 'wa')
- handed_state: float32 [32, 16, 128, 128], P('seq', 'wa')
Inputs may be any that keep to these rules, and one draw needn't show every extreme that they name: Requests lie back to back in order: request_spans[0, 0] = 0, each request's end equals the next one's start, the last end is 16384, and every request holds at least 64 tokens. The owners are distinct indices along seq; the last request's owner is the index half of 32 minus one; the first request's owner is the index just before that of the device holding the first request's last token, counted round; the index 31 is always an owner.
All inputs are finite; a program needn't handle non-finite values.
Results may differ from a plain program's by a relative error of at most 0.009.
Values may be sent and summed in bfloat16 or wider, within the bound.
No kernel may reach another device: no remote copies, remote signals or barrier semaphores. Data moves between devices by JAX's collectives and lax.ppermute only.
A program may use at most 128 MiB of HBM per device.

v0:
```python
import jax
import jax.numpy as jnp
from jax import lax
from jax.sharding import PartitionSpec as P

HEAD = 128
GROUP = 64
REQS = 4
EPS = 1e-06
HIGH = lax.Precision.HIGHEST


def entering(value, axis, join, neutral):
    count, mine = (lax.axis_size(axis), lax.axis_index(axis))
    pieces = jax.tree.map(lambda part: lax.all_gather(part, axis), value)
    so_far = jax.tree.map(
        lambda part, zero: jnp.full_like(part, 0) + jnp.asarray(zero, part.dtype), value, neutral
    )

    def hop(position, so_far):
        longer = join(so_far, jax.tree.map(lambda part: part[position], pieces))
        return jax.tree.map(lambda new, old: jnp.where(position < mine, new, old), longer, so_far)

    return lax.fori_loop(0, count - 1, hop, so_far)


def rms_rows(matrix, scaling):
    matrix = matrix.astype(jnp.float32)
    rescale = lax.rsqrt(jnp.mean(matrix * matrix, axis=-1, keepdims=True) + EPS)
    return (matrix * rescale * scaling).astype(jnp.bfloat16)


def project(matrix, weight):
    return jnp.dot(matrix, weight, preferred_element_type=jnp.float32)


def widen_rows(shard_part):
    return lax.all_gather(shard_part, "wa", axis=1, tiled=True)


def narrow_sum(partial_terms):
    return lax.psum_scatter(partial_terms, "wa", scatter_dimension=1, tiled=True)


def local(
    hidden_in,
    request_spans,
    owners,
    mixer_gain,
    query_weight,
    forget_weight,
    input_weight,
    gate_weight,
    forget_bias,
    output_weight,
    swiglu_gain,
    swiglu_gate,
    swiglu_up,
    swiglu_down,
):
    tok_rows = hidden_in.shape[0]
    head_count = query_weight.shape[1] // HEAD
    block_count = tok_rows // GROUP
    gathered = widen_rows(hidden_in)
    normed = rms_rows(gathered, mixer_gain)
    queries = jax.nn.silu(project(normed, query_weight))
    forget_logit = project(normed, forget_weight) + forget_bias
    log_decay = jax.nn.log_sigmoid(forget_logit)
    key_rows = jax.nn.sigmoid(-forget_logit)
    value_rows = project(normed, input_weight)
    gate_logit = project(normed, gate_weight)
    first_row = lax.axis_index("seq") * tok_rows
    position = first_row + jnp.arange(tok_rows, dtype=jnp.int32)
    start_rows = request_spans[:, 0]
    end_rows = request_spans[:, 1]
    is_start = jnp.any(position[:, None] == start_rows[None, :], axis=1)
    segment = jnp.sum((start_rows[None, :] <= position[:, None]).astype(jnp.int32), axis=1) - 1
    shape_four = (block_count, GROUP, head_count, HEAD)
    query_parts = queries.reshape(shape_four)
    key_parts = key_rows.reshape(shape_four)
    value_parts = value_rows.reshape(shape_four)
    segment_parts = segment.reshape(block_count, GROUP)
    keep_mask = (1.0 - is_start.astype(jnp.float32)).reshape(block_count, GROUP)
    cum_decay = jnp.cumsum(log_decay.reshape(shape_four), axis=1)
    surviving = jnp.cumprod(keep_mask, axis=1)
    query_tilde = query_parts * jnp.exp(cum_decay)
    key_tilde = key_parts * jnp.exp(-cum_decay)
    offsets = jnp.arange(GROUP, dtype=jnp.int32)
    causal = offsets[:, None] >= offsets[None, :]
    same_doc = causal[None] & (segment_parts[:, :, None] == segment_parts[:, None, :])
    scores = jnp.einsum("nihc,njhc->nhij", query_tilde, key_tilde, precision=HIGH)
    scores = jnp.where(same_doc[:, None], scores, 0.0)
    inner_out = jnp.einsum("nhij,njhd->nihd", scores, value_parts, precision=HIGH)
    tail_mask = (segment_parts == segment_parts[:, -1:]).astype(jnp.float32)
    last_decay = jnp.exp(cum_decay[:, -1])
    fresh = last_decay[..., None] * jnp.einsum(
        "njhc,njhd->nhcd", key_tilde * tail_mask[:, :, None, None], value_parts, precision=HIGH
    )
    shrink = surviving[:, -1][:, None, None] * last_decay

    def advance(carried, blocked):
        running, product = carried
        shrink_part, fresh_part = blocked
        return (
            (shrink_part[..., None] * running + fresh_part, product * shrink_part),
            (running, product),
        )

    initial = (
        jnp.zeros((head_count, HEAD, HEAD), jnp.float32),
        jnp.ones((head_count, HEAD), jnp.float32),
    )
    (local_state, device_decay), (start_state, start_decay) = lax.scan(
        advance, initial, (shrink, fresh)
    )

    def combine(earlier, follower):
        return (earlier[0] * follower[0], follower[0][..., None] * earlier[1] + follower[1])

    identity = (jnp.ones_like(device_decay), jnp.zeros_like(local_state))
    incoming = entering((device_decay, local_state), "seq", combine, identity)[1]
    block_state = start_state + start_decay[..., None] * incoming[None]
    carried_out = jnp.einsum("nihc,nhcd->nihd", query_tilde, block_state, precision=HIGH)
    mixer_out = (inner_out + surviving[:, :, None, None] * carried_out).reshape(
        tok_rows, head_count, HEAD
    )
    rescale = lax.rsqrt(jnp.mean(mixer_out * mixer_out, axis=-1, keepdims=True) + EPS)
    gate_heads = jax.nn.silu(gate_logit.reshape(tok_rows, head_count, HEAD))
    mixed_rows = (
        (mixer_out * rescale * gate_heads).reshape(tok_rows, head_count * HEAD).astype(jnp.bfloat16)
    )
    collected = []
    for request in range(REQS):
        local_end = end_rows[request] - 1 - first_row
        inside = (local_end >= 0) & (local_end < tok_rows)
        end_row = jnp.clip(local_end, 0, tok_rows - 1)
        block_index = end_row // GROUP
        within = end_row % GROUP
        decay_block = lax.dynamic_index_in_dim(cum_decay, block_index, 0, keepdims=False)
        key_block = lax.dynamic_index_in_dim(key_tilde, block_index, 0, keepdims=False)
        value_block = lax.dynamic_index_in_dim(value_parts, block_index, 0, keepdims=False)
        segment_block = lax.dynamic_index_in_dim(segment_parts, block_index, 0, keepdims=False)
        alive_block = lax.dynamic_index_in_dim(surviving, block_index, 0, keepdims=False)
        state_block = lax.dynamic_index_in_dim(block_state, block_index, 0, keepdims=False)
        decay_end = lax.dynamic_index_in_dim(decay_block, within, 0, keepdims=False)
        segment_end = lax.dynamic_index_in_dim(segment_block, within, 0, keepdims=False)
        alive_end = lax.dynamic_index_in_dim(alive_block, within, 0, keepdims=False)
        upto_mask = ((offsets <= within) & (segment_block == segment_end)).astype(jnp.float32)
        partial_end = jnp.einsum(
            "jhc,jhd->hcd", key_block * upto_mask[:, None, None], value_block, precision=HIGH
        )
        end_state = jnp.exp(decay_end)[..., None] * (alive_end * state_block + partial_end)
        collected.append(jnp.where(inside, end_state, 0.0))
    end_states = jnp.stack(collected)
    summed_states = lax.psum(end_states.astype(jnp.bfloat16), "seq").astype(jnp.float32)
    owned_mask = (owners == lax.axis_index("seq")).astype(jnp.float32)
    handed_state = jnp.einsum("r,rhcd->hcd", owned_mask, summed_states, precision=HIGH)[None]
    partial_terms = project(mixed_rows, output_weight)
    residual = (hidden_in.astype(jnp.float32) + narrow_sum(partial_terms)).astype(jnp.bfloat16)
    widened = widen_rows(residual)
    normed_ffn = rms_rows(widened, swiglu_gain)
    hidden = (
        jax.nn.silu(project(normed_ffn, swiglu_gate)) * project(normed_ffn, swiglu_up)
    ).astype(jnp.bfloat16)
    hidden_out = (residual.astype(jnp.float32) + narrow_sum(project(hidden, swiglu_down))).astype(
        jnp.bfloat16
    )
    return (hidden_out, handed_state)


def solution(mesh):
    in_specs = (
        P("seq", "wa"),
        P(),
        P(),
        P(),
        P(None, "wa"),
        P(None, "wa"),
        P(None, "wa"),
        P(None, "wa"),
        P("wa"),
        P("wa", None),
        P(),
        P(None, "wa"),
        P(None, "wa"),
        P("wa", None),
    )
    out_specs = (P("seq", "wa"), P("seq", "wa", None, None))
    return jax.shard_map(local, mesh=mesh, in_specs=in_specs, out_specs=out_specs, check_vma=False)
```

profile of v0, /device:TPU:1, one launch (start us, length us, event | category | flops | bytes accessed | tf_op | source)
XLA Modules:
  0.0 451.4 jit_solution(12406958529448473247)
XLA Ops:
  9.9 34.1 %all-gather.7.cloned.1.call-done = bf16[512,2048]{1,0:T(8,128)(2,1)} async-done(((bf16[512,512]{1,0:T(8,128)(2,1)}), bf16[512,2048]{1,0:T(8,128)(2,1)}) %all-gather.7.cloned.1.call-update) | async-done | bytes 2097168 | tf_op jit(solution)/shard_map/all_gather | solution.py:38
  44.0 2.2 fusion.1
  46.3 4.9 %add_divide_fusion = (f32[512,512]{1,0:T(8,128)}, f32[512,512]{1,0:T(8,128)}) fusion(f32[512]{0:T(512)S(1)} %copy-done.15, bf16[2048,512]{1,0:T(8,128)(2,1)} %param.23, bf16[512,2048]{1,0:T(8,128)(2,1)S(1)} %copy-done.8, f32[2048]{0:T(1024)S(1)} %copy-done.13, f32[512]{0:T(512)S(1)} %add_rsqrt_fusion.1), kind=kOutput, calls=%fused_computation.60 | convolution fusion | flops 1080819712 | bytes 6303744 | tf_op jit(solution)/shard_map/dot_general | solution.py:34
  51.2 2.5 reshape.259
  53.7 2.6 reshape.260
  56.2 4.7 %divide_multiply_fusion = f32[512,512]{1,0:T(8,128)} fusion(bf16[2048,512]{1,0:T(8,128)(2,1)} %param.22, bf16[512,2048]{1,0:T(8,128)(2,1)} %all-gather.7.cloned.1.call-done, f32[2048]{0:T(1024)S(1)} %copy-done.13, f32[512]{0:T(512)S(1)} %add_rsqrt_fusion.1), kind=kOutput, calls=%fused_computation.61 | convolution fusion | flops 1078984704 | bytes 5253120 | tf_op jit(solution)/shard_map/dot_general | solution.py:34
  61.0 2.5 reshape.258
  63.5 4.9 %broadcast_multiply_fusion = (f32[8,64,4,128]{3,0,1,2:T(8,128)}, f32[8,64,4,128]{3,0,1,2:T(8,128)}, f32[8,64,4,128]{3,0,1,2:T(8,128)}, f32[8,64,4,128]{3,0,1,2:T(8,128)S(1)}) fusion(f32[8,64]{0,1:T(8,128)S(1)} %copy.108, f32[8,64,4,128]{3,2,1,0:T(4,128)} %reshape.260, f32[8,64,4,128]{3,2,1,0:T(4,128)} %reshape.258, f32[8,64,4,128]{3,2,1,0:T(4,128)} %reshape.259), kind=kOutput, calls=%fused_computation.70 | output fusion | flops 17563648 | bytes 7342080 | tf_op jit(solution)/shard_map/jit(cumsum)/reduce_window_sum | solution.py:84
  69.4 2.3 fusion.80
  71.6 2.5 reshape.257
  75.0 6.8 %convolution_multiply_fusion = f32[8,4,128,128]{3,2,1,0:T(8,128)} fusion(f32[8,64,4,128]{3,0,1,2:T(8,128)} %get-tuple-element.249, f32[8,4,128]{2,1,0:T(4,128)S(1)} %copy.107, f32[8,64,4,128]{3,2,1,0:T(4,128)} %reshape.257), kind=kOutput, calls=%fused_computation.20 | convolution fusion | flops 403177472 | bytes 4210688 | tf_op jit(solution)/shard_map/njhc,njhd->nhcd/dot_general | solution.py:96
  81.8 15.2 %while.31 = (s32[]{:T(128)}, f32[4,128,128]{2,1,0:T(8,128)S(1)}, f32[4,128]{1,0:T(4,128)S(1)}, f32[8,4,128,128]{3,2,1,0:T(8,128)}, f32[8,4,128]{2,1,0:T(4,128)S(...) while((s32[]{:T(128)}, f32[4,128,128]{2,1,0:T(8,128)S(1)}, ...), condition=%wide.region_6.7_spmd.clone, body=%wide.region_5.6_spmd.clone.sunk | while | flops 263683 | bytes 1327734 | solution.py:113
  98.0 24.7 %all-gather.2 = f32[32,4,128]{2,1,0:T(4,128)S(1)} all-gather(f32[1,4,128]{2,1,0:T(4,128)S(1)} %bitcast.142), channel_id=2, replica_groups=mesh['seq'=32,'wa'=4] {'seq'}, dimensions={0}, use_global_device_ids=true | all-gather | bytes 67584 | tf_op jit(solution)/shard_map/all_gather | solution.py:15
  122.6 4.5 %convolution_select_fusion = f32[8,4,64,64]{3,2,1,0:T(8,128)} fusion(f32[8,64,4,128]{3,0,1,2:T(8,128)} %get-tuple-element.250, f32[8,64,4,128]{3,0,1,2:T(8,128)} %get-tuple-element.263, pred[8,64,64]{2,1,0:T(8,128)(4,1)S(1)} %compare_and_fusion), kind=kOutput, calls=%fused_computation.25 | convolution fusion | flops 201457664 | bytes 2654208 | tf_op jit(solution)/shard_map/nihc,njhc->nhij/dot_general | solution.py:91
  127.2 23.8 %all-gather.11.cloned.1.call-done = f32[128,128,128]{2,1,0:T(8,128)} async-done(((f32[4,128,128]{2,1,0:T(8,128)}), f32[128,128,128]{2,1,0:T(8,128)}) %all-gather.11.cloned.1.call-update) | async-done | bytes 8388624 | tf_op jit(solution)/shard_map/all_gather | solution.py:15
  151.0 37.0 %while.32 = (s32[]{:T(128)}, f32[4,128,128]{2,1,0:T(8,128)S(1)}, s32[]{:T(128)}, f32[32,4,128]{2,1,0:T(4,128)S(1)}, f32[32,4,128,128]{3,2,1,0:T(8,128)}, /*index=5*/s32[]{:T(128)}, s32[]{:T(128)}) while((s32[]{:T(128)}, f32[4,128,128]{2,1,0:T(8,128)S(1)}, s32[]{:T(128)}, f32[32,4,128]{2,1,0:T(4,128)S(1)}, ...), condition=%wide.region_8.9_spmd.clone, body=%wide.region_7.8_spmd.clone.sunk | while | flops 262148 | bytes 792681 | solution.py:24
  157.0 1.1 fusion.102
  158.1 1.1 fusion.102
  159.3 1.1 fusion.102
  160.5 1.1 fusion.102
  168.9 1.1 fusion.102
  170.1 1.1 fusion.102
  171.3 1.1 fusion.102
  179.6 1.1 fusion.102
  180.8 1.1 fusion.102
  182.0 1.1 fusion.102
  188.0 2.0 multiply_add_fusion
  190.0 2.0 convolution_multiply_fusion.1
  192.3 2.2 multiply_reduce_fusion
  194.7 2.9 copy.113
  197.6 1.6 mul.291
  199.2 8.0 %fusion.40 = f32[512,2048]{1,0:T(8,128)} fusion(bf16[512,2048]{1,0:T(8,128)(2,1)} %param.27, f32[64,8,4,128]{3,2,1,0:T(4,128)} %bitcast.133, f32[64,8,4,128]{3,2,1,0:T(4,128)} %bitcast.135, bf16[2048,512]{1,0:T(8,128)(2,1)} %param.25, bf16[512,2048]{1,0:T(8,128)(2,1)} %all-gather.7.cloned.1.call-done, f32[2048]{0:T(1024)S(1)} %copy-done.13, ...), kind=kOutput, calls=%fused_computation.68 | convolution fusion | flops 2153512960 | bytes 12593152 | tf_op jit(solution)/shard_map/dot_general | solution.py:34
  207.3 46.4 %reduce-scatter.3.cloned.1.call-done = f32[512,512]{1,0:T(8,128)} async-done(((f32[512,2048]{1,0:T(8,128)}), f32[512,512]{1,0:T(8,128)}) %reduce-scatter.3.cloned.1.call-update) | async-done | bytes 1048592 | tf_op jit(solution)/shard_map/reduce_scatter | solution.py:42
  253.7 2.3 add_convert_fusion.1
  260.6 2.4 fusion.71
  263.9 3.2 constant_dynamic-slice_fusion.15
  268.2 1.3 fusion.23
  269.6 1.3 fusion.22
  270.8 1.3 fusion.21
  272.1 1.3 fusion.20
  274.4 12.3 %all-gather.9.cloned.1.call-done = bf16[512,2048]{1,0:T(8,128)(2,1)} async-done(((bf16[512,512]{1,0:T(8,128)(2,1)}), bf16[512,2048]{1,0:T(8,128)(2,1)}) %all-gather.9.cloned.1.call-update) | async-done | bytes 2097168 | tf_op jit(solution)/shard_map/all_gather | solution.py:38
  286.8 2.2 fusion.4
  289.0 5.0 %fusion.38 = f32[512,768]{1,0:T(8,128)} fusion(bf16[2048,768]{1,0:T(8,128)(2,1)} %param.29, bf16[512,2048]{1,0:T(8,128)(2,1)S(1)} %copy-done.7, f32[2048]{0:T(1024)S(1)} %copy-done.14, f32[512]{0:T(512)S(1)} %add_rsqrt_fusion), kind=kOutput, calls=%fused_computation.67 | convolution fusion | flops 1614807040 | bytes 6825984 | tf_op jit(solution)/shard_map/dot_general | solution.py:34
  294.0 8.9 %fusion.35 = f32[512,2048]{1,0:T(8,128)} fusion(bf16[768,2048]{1,0:T(8,128)(2,1)S(1)} %copy-done, f32[512,768]{1,0:T(8,128)} %fusion.38, bf16[2048,768]{1,0:T(8,128)(2,1)} %param.30, bf16[512,2048]{1,0:T(8,128)(2,1)} %all-gather.9.cloned.1.call-done, f32[2048]{0:T(1024)S(1)} %copy-done.14, f32[512]{0:T(512)S(1)} %add_rsqrt_fusion), kind=kOutput, calls=%fused_computation.66 | convolution fusion | flops 3227779072 | bytes 14166016 | tf_op jit(solution)/shard_map/dot_general | solution.py:34
  302.9 90.3 %all-reduce.2.cloned.1.call-done = bf16[4,4,128,128]{3,2,1,0:T(8,128)(2,1)} async-done(((bf16[4,4,128,128]{3,2,1,0:T(8,128)(2,1)}), bf16[4,4,128,128]{3,2,1,0:T(8,128)(2,1)}) %all-reduce.2.cloned.1.call-update) | async-done | bytes 524304 | tf_op jit(solution)/shard_map/psum | solution.py:155
  393.3 2.2 fusion.43
  395.5 46.7 %reduce-scatter.5.cloned.1.call-done = f32[512,512]{1,0:T(8,128)} async-done(((f32[512,2048]{1,0:T(8,128)}), f32[512,512]{1,0:T(8,128)}) %reduce-scatter.5.cloned.1.call-update) | async-done | bytes 1048592 | tf_op jit(solution)/shard_map/reduce_scatter | solution.py:42
  442.2 2.3 add_convert_fusion
  (171 shorter events, 50.2 us)
Async XLA Ops:
  7.2 286.8 %copy-start = (bf16[768,2048]{1,0:T(8,128)(2,1)S(1)}, bf16[768,2048]{1,0:T(8,128)(2,1)}, u32[]{:S(2)}) copy-start(bf16[768,2048]{1,0:T(8,128)(2,1)} %param.31) | copy-start | bytes 9437188
  7.2 39.1 %copy-start.13 = (f32[2048]{0:T(1024)S(1)}, f32[2048]{0:T(1024)}, u32[]{:S(2)}) copy-start(f32[2048]{0:T(1024)} %param.21) | copy-start | bytes 24580
  7.2 39.1 %copy-start.15 = (f32[512]{0:T(512)S(1)}, f32[512]{0:T(512)}, u32[]{:S(2)}) copy-start(f32[512]{0:T(512)} %param.26) | copy-start | bytes 6148
  7.2 36.8 %all-gather.7.cloned.1.call-start = ((), (), s32[]{:S(2)}) async-start(), calls=%async_computation.2 | async-start | bytes 2621440 | tf_op jit(solution)/shard_map/all_gather | solution.py:38
  7.9 143.1 %all-gather.11.cloned.1.call-start = ((), (), s32[]{:S(2)}) async-start(), calls=%async_computation.7 | async-start | bytes 8650752 | tf_op jit(solution)/shard_map/all_gather | solution.py:15
  44.0 2.3 copy-start.8
  63.5 5.9 %copy-start.9 = (bf16[512,2048]{1,0:T(8,128)(2,1)S(1)}, bf16[512,2048]{1,0:T(8,128)(2,1)}, u32[]{:S(2)}) copy-start(bf16[512,2048]{1,0:T(8,128)(2,1)} %all-gather.7.cloned.1.call-done) | copy-start | bytes 6291460
  63.5 5.9 %copy-start.12 = (bf16[2048,512]{1,0:T(8,128)(2,1)S(1)}, bf16[2048,512]{1,0:T(8,128)(2,1)}, u32[]{:S(2)}) copy-start(bf16[2048,512]{1,0:T(8,128)(2,1)} %param.24) | copy-start | bytes 6291460
  68.4 1.0 copy-start.10
  97.0 0.7 copy-start.1
  97.8 155.9 %reduce-scatter.3.cloned.1.call-start = ((), (), s32[]{:S(2)}) async-start(), calls=%async_computation.3 | async-start | bytes 5242880 | tf_op jit(solution)/shard_map/reduce_scatter | solution.py:42
  187.9 2.1 copy-start.5
  190.0 2.1 copy-start.2
  190.0 2.1 copy-start.4
  190.0 2.3 copy-start.6
  207.2 49.0 %copy-start.11 = (s32[4,2]{0,1:T(2,128)S(1)}, s32[4,2]{0,1:T(2,128)}, u32[]{:S(2)}) copy-start(s32[4,2]{0,1:T(2,128)} %param.19) | copy-start | bytes 100
  207.2 79.5 %all-gather.9.cloned.1.call-start = ((), (), s32[]{:S(2)}) async-start(), calls=%async_computation.4 | async-start | bytes 2621440 | tf_op jit(solution)/shard_map/all_gather | solution.py:38
  256.0 137.3 %all-reduce.2.cloned.1.call-start = ((), (), s32[]{:S(2)}) async-start(), calls=%async_computation.6 | async-start | bytes 1048576 | tf_op jit(solution)/shard_map/psum | solution.py:155
  259.4 8.8 %copy-start.3 = (f32[8,4,128,128]{3,2,1,0:T(8,128)S(1)}, f32[8,4,128,128]{3,2,1,0:T(8,128)}, u32[]{:S(2)}) copy-start(f32[8,4,128,128]{3,2,1,0:T(8,128)} %copy-done.2) | copy-start | bytes 6291460
  272.1 16.9 %copy-start.14 = (f32[2048]{0:T(1024)S(1)}, f32[2048]{0:T(1024)}, u32[]{:S(2)}) copy-start(f32[2048]{0:T(1024)} %param.28) | copy-start | bytes 24580
  274.4 167.9 %reduce-scatter.5.cloned.1.call-start = ((), (), s32[]{:S(2)}) async-start(), calls=%async_computation.5 | async-start | bytes 5242880 | tf_op jit(solution)/shard_map/reduce_scatter | solution.py:42
  286.7 2.2 copy-start.7
  302.9 90.4 %copy-start.16 = (s32[4]{0:T(128)S(1)}, s32[4]{0:T(128)}, u32[]{:S(2)}) copy-start(s32[4]{0:T(128)} %param.20) | copy-start | bytes 52
Sparse Core Ops, SparseCore 0:
  9.7 34.2 all-gather.6
  97.9 53.0 all-gather.10
  207.4 46.2 reduce-scatter.2
  256.1 30.5 all-gather.8
  290.1 103.1 all-reduce.1
  395.5 46.6 reduce-scatter.4
where the time goes:
time: 453 us; the launch traced here: 451 us
  waiting for transfers between devices  254 us (56%)
  other arithmetic  71.2 us (16%)
  matrix products  56.8 us (13%)
  local copies, waits for them, and re-layouts  25.5 us (6%)
  blocking collectives  24.7 us (5%)
  between operations  17 us (4%)
    reduce_scatter x2, waiting for transfers between devices, narrow_sum(): lax.psum_scatter(partial_terms, 'wa', scatter_dimension=1, tiled=True)  93.1 us
    psum x1, waiting for transfers between devices, local(): lax.psum(end_states.astype(jnp.bfloat16), 'seq').astype(jnp.float32)  90.3 us
    all_gather x2, waiting for transfers between devices, widen_rows(): return lax.all_gather(shard_part, 'wa', axis=1, tiled=True)  46.4 us
    select_n x31, other arithmetic, hop(): jnp.where(position < mine, new, old)  35.6 us
    dot_general x6, matrix products, project(): return jnp.dot(matrix, weight, preferred_element_type=jnp.float32)  33.8 us
    all_gather x1, blocking collectives, entering(): pieces = jax.tree.map(lambda part: lax.all_gather(part, axis), value)  24.7 us
    all_gather x1, waiting for transfers between devices, entering(): pieces = jax.tree.map(lambda part: lax.all_gather(part, axis), value)  23.8 us
  transfers between devices with their start and end apart: 6, of which 6 were waited for; matrix products, arithmetic and copies ran while one was open for 9% of the time, Pallas kernels for 0%

commit v1 on v0

--- a/solution.py
+++ b/solution.py
@@ -10,6 +10,25 @@
 HIGH = lax.Precision.HIGHEST
 
 
+def ring_gather(array, axis, dim):
+    size, mine, rows = (lax.axis_size(axis), lax.axis_index(axis), array.shape[dim])
+    forward = [(i, (i + 1) % size) for i in range(size)]
+    left = [(i, (i - 1) % size) for i in range(size)]
+    out = jnp.zeros((*array.shape[:dim], size * rows, *array.shape[dim + 1 :]), array.dtype)
+    out = lax.dynamic_update_slice_in_dim(out, array, mine * rows, axis=dim)
+    from_left = from_right = array
+    halfway = size // 2
+    for lap in range(1, halfway + 1):
+        from_left = lax.ppermute(from_left, axis, forward)
+        out = lax.dynamic_update_slice_in_dim(out, from_left, (mine - lap) % size * rows, axis=dim)
+        if lap < size - halfway:
+            from_right = lax.ppermute(from_right, axis, left)
+            out = lax.dynamic_update_slice_in_dim(
+                out, from_right, (mine + lap) % size * rows, axis=dim
+            )
+    return out
+
+
 def entering(value, axis, join, neutral):
     count, mine = (lax.axis_size(axis), lax.axis_index(axis))
     pieces = jax.tree.map(lambda part: lax.all_gather(part, axis), value)
@@ -35,7 +54,7 @@
 
 
 def widen_rows(shard_part):
-    return lax.all_gather(shard_part, "wa", axis=1, tiled=True)
+    return ring_gather(shard_part, "wa", 1)
 
 
 def narrow_sum(partial_terms):

time: 453 us -> 433 us (0.956)
  waiting for transfers between devices: 254 us -> 221 us
  local copies, waits for them, and re-layouts: 25.5 us -> 33.8 us
  starting transfers between devices: 0.46 us -> 7.54 us
    all_gather x2 -> x0, waiting for transfers between devices: 46.4 us -> none  [widen_rows(): return lax.all_gather(shard_part, 'wa', axis=1, tiled=True)]
    ppermute x0 -> x6, waiting for transfers between devices: none -> 33.7 us  [the longest x4 33.7 us: ring_gather(): from_left = lax.ppermute(from_left, axis, forward)]
    psum x1, waiting for transfers between devices: 90.3 us -> 79.5 us  [local(): lax.psum(end_states.astype(jnp.bfloat16), 'seq').astype(jnp.float32)]
    dynamic_update_slice x0 -> x7, local copies, waits for them, and re-layouts: none -> 9.48 us  [the longest x4 6.26 us: ring_gather(): lax.dynamic_update_slice_in_dim(out, from_left, (mine - lap) % size * row...]
    reduce_scatter x2, waiting for transfers between devices: 93.1 us -> 85.1 us  [narrow_sum(): lax.psum_scatter(partial_terms, 'wa', scatter_dimension=1, tiled=True)]
    ppermute x0 -> x6, starting transfers between devices: none -> 7.37 us  [the longest x2 4.83 us: ring_gather(): from_right = lax.ppermute(from_right, axis, left)]
  transfers between devices with their start and end apart: 6 -> 10, of which waited for: 6 -> 8; matrix products, arithmetic and copies ran while one was open for 9% -> 10% of each run, Pallas kernels for 0% -> 0%
where the time goes in v1:
time: 433 us; the launch traced here: 431 us
  waiting for transfers between devices  221 us (51%)
  other arithmetic  69.1 us (16%)
  matrix products  54.4 us (13%)
  local copies, waits for them, and re-layouts  33.8 us (8%)
  blocking collectives  26.4 us (6%)
  between operations  17 us (4%)
  starting transfers between devices  7.54 us (2%)
    reduce_scatter x2, waiting for transfers between devices, narrow_sum(): lax.psum_scatter(partial_terms, 'wa', scatter_dimension=1, tiled=True)  85.1 us
    psum x1, waiting for transfers between devices, local(): lax.psum(end_states.astype(jnp.bfloat16), 'seq').astype(jnp.float32)  79.5 us
    select_n x31, other arithmetic, hop(): jnp.where(position < mine, new, old)  35.6 us
    ppermute x4, waiting for transfers between devices, ring_gather(): from_left = lax.ppermute(from_left, axis, forward)  33.7 us
    dot_general x6, matrix products, project(): return jnp.dot(matrix, weight, preferred_element_type=jnp.float32)  32.5 us
    all_gather x1, blocking collectives, entering(): pieces = jax.tree.map(lambda part: lax.all_gather(part, axis), value)  26.4 us
    all_gather x1, waiting for transfers between devices, entering(): pieces = jax.tree.map(lambda part: lax.all_gather(part, axis), value)  22.5 us
    add x8, other arithmetic, advance(): shrink_part[..., None] * running + fresh_part  8.93 us
  transfers between devices with their start and end apart: 10, of which 8 were waited for; matrix products, arithmetic and copies ran while one was open for 10% of the time, Pallas kernels for 0%

profile of v1, /device:TPU:1, one launch (start us, length us, event | category | flops | bytes accessed | tf_op | source)
XLA Modules:
  0.0 430.6 jit_solution(7104493795805165086)
XLA Ops:
  7.2 2.5 collective-permute-start
  9.8 2.2 collective-permute-start.1
  13.2 10.7 %collective-permute-done = bf16[512,512]{1,0:T(8,128)(2,1)} collective-permute-done((bf16[512,512]{1,0:T(8,128)(2,1)}, bf16[512,512]{1,0:T(8,128)(2,1)}, u32[]{:S(2)}, u32[]{:S(2)}) %collective-permute-start) | collective-permute-done | bytes 524320 | tf_op jit(solution)/shard_map/ppermute | solution.py:22
  26.5 1.2 constant_dynamic-update-slice_fusion.5
  27.8 9.8 %collective-permute-done.2 = bf16[512,512]{1,0:T(8,128)(2,1)} collective-permute-done((bf16[512,512]{1,0:T(8,128)(2,1)}, bf16[512,512]{1,0:T(8,128)(2,1)}, u32[]{:S(2)}, u32[]{:S(2)}) %collective-permute-start.2) | collective-permute-done | bytes 524320 | tf_op jit(solution)/shard_map/ppermute | solution.py:22
  40.1 2.3 fusion.80
  42.4 2.6 reshape.257
  44.9 4.6 %divide_multiply_fusion = f32[512,512]{1,0:T(8,128)} fusion(bf16[2048,512]{1,0:T(8,128)(2,1)} %param.22, bf16[512,2048]{1,0:T(8,128)(2,1)} %copy-done.10, f32[2048]{0:T(1024)S(1)} %copy-done.19, f32[512]{0:T(512)S(1)} %add_rsqrt_fusion.1), kind=kOutput, calls=%fused_computation.61 | convolution fusion | flops 1078984704 | bytes 5253120 | tf_op jit(solution)/shard_map/dot_general | solution.py:53
  49.6 2.6 reshape.258
  52.2 5.5 %add_divide_fusion = (f32[512,512]{1,0:T(8,128)}, f32[512,512]{1,0:T(8,128)}) fusion(f32[512]{0:T(512)S(1)} %copy-done.21, bf16[2048,512]{1,0:T(8,128)(2,1)} %param.23, bf16[512,2048]{1,0:T(8,128)(2,1)} %copy-done.10, f32[2048]{0:T(1024)S(1)} %copy-done.19, f32[512]{0:T(512)S(1)} %add_rsqrt_fusion.1), kind=kOutput, calls=%fused_computation.60 | convolution fusion | flops 1080819712 | bytes 6303744 | tf_op jit(solution)/shard_map/dot_general | solution.py:53
  57.7 2.5 reshape.259
  60.2 2.6 reshape.260
  62.8 4.9 %broadcast_multiply_fusion = (f32[8,64,4,128]{3,0,1,2:T(8,128)S(1)}, f32[8,64,4,128]{3,0,1,2:T(8,128)}, f32[8,64,4,128]{3,0,1,2:T(8,128)}, f32[8,64,4,128]{3,0,1,2:T(8,128)S(1)}) fusion(f32[8,64]{0,1:T(8,128)S(1)} %copy.108, f32[8,64,4,128]{3,2,1,0:T(4,128)} %reshape.260, f32[8,64,4,128]{3,2,1,0:T(4,128)} %reshape.258, f32[8,64,4,128]{3,2,1,0:T(4,128)} %reshape.259), kind=kOutput, calls=%fused_computation.70 | output fusion | flops 17563648 | bytes 7342080 | tf_op jit(solution)/shard_map/jit(cumsum)/reduce_window_sum | solution.py:103
  67.8 5.5 %convolution_multiply_fusion = f32[8,4,128,128]{3,2,1,0:T(8,128)} fusion(f32[8,64,4,128]{3,0,1,2:T(8,128)S(1)} %get-tuple-element.251, f32[8,4,128]{2,1,0:T(4,128)S(1)} %copy.107, f32[8,64,4,128]{3,2,1,0:T(4,128)S(1)} %copy-done.4), kind=kOutput, calls=%fused_computation.20 | convolution fusion | flops 403177472 | bytes 4210688 | tf_op jit(solution)/shard_map/njhc,njhd->nhcd/dot_general | solution.py:115
  73.2 15.2 %while.31 = (s32[]{:T(128)}, f32[4,128,128]{2,1,0:T(8,128)S(1)}, f32[4,128]{1,0:T(4,128)S(1)}, f32[8,4,128,128]{3,2,1,0:T(8,128)}, f32[8,4,128]{2,1,0:T(4,128)S(...) while((s32[]{:T(128)}, f32[4,128,128]{2,1,0:T(8,128)S(1)}, ...), condition=%wide.region_6.7_spmd.clone, body=%wide.region_5.6_spmd.clone.sunk | while | flops 263683 | bytes 1327734 | solution.py:132
  89.4 26.4 %all-gather.2 = f32[32,4,128]{2,1,0:T(4,128)S(1)} all-gather(f32[1,4,128]{2,1,0:T(4,128)S(1)} %bitcast.142), channel_id=2, replica_groups=mesh['seq'=32,'wa'=4] {'seq'}, dimensions={0}, use_global_device_ids=true | all-gather | bytes 67584 | tf_op jit(solution)/shard_map/all_gather | solution.py:34
  115.9 4.5 %convolution_select_fusion = f32[8,4,64,64]{3,2,1,0:T(8,128)} fusion(f32[8,64,4,128]{3,0,1,2:T(8,128)} %get-tuple-element.252, f32[8,64,4,128]{3,0,1,2:T(8,128)} %get-tuple-element.265, pred[8,64,64]{2,1,0:T(8,128)(4,1)S(1)} %compare_and_fusion), kind=kOutput, calls=%fused_computation.25 | convolution fusion | flops 201457664 | bytes 2654208 | tf_op jit(solution)/shard_map/nihc,njhc->nhij/dot_general | solution.py:110
  120.4 22.5 %all-gather.5.cloned.1.call-done = f32[128,128,128]{2,1,0:T(8,128)} async-done(((f32[4,128,128]{2,1,0:T(8,128)}), f32[128,128,128]{2,1,0:T(8,128)}) %all-gather.5.cloned.1.call-update) | async-done | bytes 8388624 | tf_op jit(solution)/shard_map/all_gather | solution.py:34
  142.9 37.0 %while.32 = (s32[]{:T(128)}, f32[4,128,128]{2,1,0:T(8,128)S(1)}, s32[]{:T(128)}, f32[32,4,128]{2,1,0:T(4,128)S(1)}, f32[32,4,128,128]{3,2,1,0:T(8,128)}, /*index=5*/s32[]{:T(128)}, s32[]{:T(128)}) while((s32[]{:T(128)}, f32[4,128,128]{2,1,0:T(8,128)S(1)}, s32[]{:T(128)}, f32[32,4,128]{2,1,0:T(4,128)S(1)}, ...), condition=%wide.region_8.9_spmd.clone, body=%wide.region_7.8_spmd.clone.sunk | while | flops 262148 | bytes 792681 | solution.py:43
  146.5 1.1 fusion.102
  151.3 1.1 fusion.102
  152.5 1.1 fusion.102
  179.9 2.0 multiply_add_fusion
  182.0 2.0 convolution_multiply_fusion.1
  184.3 2.2 multiply_reduce_fusion
  186.7 2.9 copy.113
  189.6 1.6 mul.311
  191.2 8.0 %fusion.40 = f32[512,2048]{1,0:T(8,128)} fusion(bf16[512,2048]{1,0:T(8,128)(2,1)} %param.27, f32[64,8,4,128]{3,2,1,0:T(4,128)} %bitcast.133, f32[64,8,4,128]{3,2,1,0:T(4,128)} %bitcast.135, bf16[2048,512]{1,0:T(8,128)(2,1)} %param.25, bf16[512,2048]{1,0:T(8,128)(2,1)} %copy-done.10, f32[2048]{0:T(1024)S(1)} %copy-done.19, f32[512]{0:T(512)S(1)} %add_rsqrt_fusion.1), kind=kOutput, calls=%fused_computation.68 | convolution fusion | flops 2153512960 | bytes 12593152 | tf_op jit(solution)/shard_map/dot_general | solution.py:53
  204.7 2.6 fusion.71
  207.3 38.4 %reduce-scatter.3.cloned.1.call-done = f32[512,512]{1,0:T(8,128)} async-done(((f32[512,2048]{1,0:T(8,128)}), f32[512,512]{1,0:T(8,128)}) %reduce-scatter.3.cloned.1.call-update) | async-done | bytes 1048592 | tf_op jit(solution)/shard_map/reduce_scatter | solution.py:61
  246.7 2.4 constant_dynamic-update-slice_fusion.3
  250.6 1.4 fusion.23
  252.0 2.6 collective-permute-start.4
  254.6 1.3 fusion.22
  255.9 7.6 %collective-permute-done.3 = bf16[512,512]{1,0:T(8,128)(2,1)} collective-permute-done((bf16[512,512]{1,0:T(8,128)(2,1)}, bf16[512,512]{1,0:T(8,128)(2,1)}, u32[]{:S(2)}, u32[]{:S(2)}) %collective-permute-start.3) | collective-permute-done | bytes 524320 | tf_op jit(solution)/shard_map/ppermute | solution.py:22
  263.5 1.4 fusion.21
  264.9 1.4 fusion.20
  267.3 2.1 constant_dynamic-update-slice_fusion.2
  269.4 1.9 constant_dynamic-update-slice_fusion.1
  271.4 5.6 %collective-permute-done.5 = bf16[512,512]{1,0:T(8,128)(2,1)} collective-permute-done((bf16[512,512]{1,0:T(8,128)(2,1)}, bf16[512,512]{1,0:T(8,128)(2,1)}, u32[]{:S(2)}, u32[]{:S(2)}) %collective-permute-start.5) | collective-permute-done | bytes 524320 | tf_op jit(solution)/shard_map/ppermute | solution.py:22
  277.0 1.9 constant_dynamic-update-slice_fusion
  279.0 2.2 fusion.4
  281.2 3.1 fusion.38
  284.3 9.0 %fusion.35 = f32[512,2048]{1,0:T(8,128)} fusion(bf16[768,2048]{1,0:T(8,128)(2,1)S(1)} %copy-done, f32[512,768]{1,0:T(8,128)} %fusion.38, bf16[2048,768]{1,0:T(8,128)(2,1)} %param.30, bf16[512,2048]{1,0:T(8,128)(2,1)} %constant_dynamic-update-slice_fusion, f32[2048]{0:T(1024)S(1)} %copy-done.20, f32[512]{0:T(512)S(1)} %add_rsqrt_fusion), kind=kOutput, calls=%fused_computation.66 | convolution fusion | flops 3227779072 | bytes 14166016 | tf_op jit(solution)/shard_map/dot_general | solution.py:53
  293.3 79.5 %all-reduce.2.cloned.1.call-done = bf16[4,4,128,128]{3,2,1,0:T(8,128)(2,1)} async-done(((bf16[4,4,128,128]{3,2,1,0:T(8,128)(2,1)}), bf16[4,4,128,128]{3,2,1,0:T(8,128)(2,1)}) %all-reduce.2.cloned.1.call-update) | async-done | bytes 524304 | tf_op jit(solution)/shard_map/psum | solution.py:174
  372.8 2.2 fusion.43
  375.0 46.7 %reduce-scatter.5.cloned.1.call-done = f32[512,512]{1,0:T(8,128)} async-done(((f32[512,2048]{1,0:T(8,128)}), f32[512,512]{1,0:T(8,128)}) %reduce-scatter.5.cloned.1.call-update) | async-done | bytes 1048592 | tf_op jit(solution)/shard_map/reduce_scatter | solution.py:61
  421.7 2.3 add_convert_fusion
  (198 shorter events, 61.3 us)
Async XLA Ops:
  7.2 277.1 %copy-start = (bf16[768,2048]{1,0:T(8,128)(2,1)S(1)}, bf16[768,2048]{1,0:T(8,128)(2,1)}, u32[]{:S(2)}) copy-start(bf16[768,2048]{1,0:T(8,128)(2,1)} %param.31) | copy-start | bytes 9437188
  7.2 135.8 %all-gather.5.cloned.1.call-start = ((), (), s32[]{:S(2)}) async-start(), calls=%async_computation.5 | async-start | bytes 8650752 | tf_op jit(solution)/shard_map/all_gather | solution.py:34
  7.2 16.6 %collective-permute-start = (bf16[512,512]{1,0:T(8,128)(2,1)}, bf16[512,512]{1,0:T(8,128)(2,1)}, u32[]{:S(2)}, u32[]{:S(2)}) collective-permute-start(bf16[512,512]{1,0:T(8,128)(2,1)} %param.18), channel_id=1, source_target_pairs={{0,1},{1,2},{2,3},{3,0},{4,5},{5,6},{6,7},{7,4},{8,9},{9,10},{10,1... | collective-permute-start | bytes 1572872 | tf_op jit(solution)/shard_map/ppermute | solution.py:22
  9.8 16.8 %collective-permute-start.1 = (bf16[512,512]{1,0:T(8,128)(2,1)}, bf16[512,512]{1,0:T(8,128)(2,1)}, u32[]{:S(2)}, u32[]{:S(2)}) collective-permute-start(bf16[512,512]{1,0:T(8,128)(2,1)} %param.18), channel_id=1, source_target_pairs={{0,3},{1,0},{2,1},{3,2},{4,7},{5,4},{6,5},{7,6},{8,11},{9,8},{10,9... | collective-permute-start | bytes 1572872 | tf_op jit(solution)/shard_map/ppermute | solution.py:25
  23.8 13.7 %collective-permute-start.2 = (bf16[512,512]{1,0:T(8,128)(2,1)}, bf16[512,512]{1,0:T(8,128)(2,1)}, u32[]{:S(2)}, u32[]{:S(2)}) collective-permute-start(bf16[512,512]{1,0:T(8,128)(2,1)} %collective-permute-done), channel_id=1, source_target_pairs={{0,1},{1,2},{2,3},{3,0},{4,5},{5,6},{6,7},{7,4},{8,9},{9,10},{10,1... | collective-permute-start | bytes 1572872 | tf_op jit(solution)/shard_map/ppermute | solution.py:22
  24.3 1.0 copy-start.13
  26.5 13.6 %copy-start.18 = (bf16[2048,512]{1,0:T(8,128)(2,1)S(1)}, bf16[2048,512]{1,0:T(8,128)(2,1)}, u32[]{:S(2)}) copy-start(bf16[2048,512]{1,0:T(8,128)(2,1)} %param.24) | copy-start | bytes 6291460
  26.5 13.6 %copy-start.19 = (f32[2048]{0:T(1024)S(1)}, f32[2048]{0:T(1024)}, u32[]{:S(2)}) copy-start(f32[2048]{0:T(1024)} %param.21) | copy-start | bytes 24580
  38.7 1.4 copy-start.10
  49.6 2.6 copy-start.21
  62.8 5.0 %copy-start.4 = (f32[8,64,4,128]{3,2,1,0:T(4,128)S(1)}, f32[8,64,4,128]{3,2,1,0:T(4,128)}, u32[]{:S(2)}) copy-start(f32[8,64,4,128]{3,2,1,0:T(4,128)} %reshape.257) | copy-start | bytes 3145732
  67.7 5.6 %copy-start.15 = (f32[8,64,4,128]{3,0,1,2:T(8,128)}, f32[8,64,4,128]{3,0,1,2:T(8,128)S(1)}, u32[]{:S(2)}) copy-start(f32[8,64,4,128]{3,0,1,2:T(8,128)S(1)} %get-tuple-element.284) | copy-start | bytes 3145732
  88.5 0.7 copy-start.1
  89.2 156.5 %reduce-scatter.3.cloned.1.call-start = ((), (), s32[]{:S(2)}) async-start(), calls=%async_computation.2 | async-start | bytes 5242880 | tf_op jit(solution)/shard_map/reduce_scatter | solution.py:61
  179.9 2.1 copy-start.7
  182.0 2.1 copy-start.2
  182.0 2.1 copy-start.5
  182.0 2.3 copy-start.12
  199.2 0.7 copy-start.16
  199.2 173.5 %all-reduce.2.cloned.1.call-start = ((), (), s32[]{:S(2)}) async-start(), calls=%async_computation.4 | async-start | bytes 1048576 | tf_op jit(solution)/shard_map/psum | solution.py:174
  245.7 1.0 copy-start.14
  245.7 4.4 %copy-start.6 = (f32[8,64,4,128]{3,2,1,0:T(4,128)S(1)}, f32[8,64,4,128]{3,2,1,0:T(4,128)}, u32[]{:S(2)}) copy-start(f32[8,64,4,128]{3,2,1,0:T(4,128)} %reshape.257) | copy-start | bytes 3145732
  246.7 3.4 copy-start.11
  246.7 3.9 copy-start.3
  249.1 17.2 %copy-start.8 = (bf16[512,2048]{1,0:T(8,128)(2,1)}, bf16[512,2048]{1,0:T(8,128)(2,1)S(1)}, u32[]{:S(2)}) copy-start(bf16[512,2048]{1,0:T(8,128)(2,1)S(1)} %get-tuple-element.249) | copy-start | bytes 6291460
  249.1 14.4 %collective-permute-start.3 = (bf16[512,512]{1,0:T(8,128)(2,1)}, bf16[512,512]{1,0:T(8,128)(2,1)}, u32[]{:S(2)}, u32[]{:S(2)}) collective-permute-start(bf16[512,512]{1,0:T(8,128)(2,1)} %get-tuple-element.250), channel_id=1, source_target_pairs={{0,1},{1,2},{2,3},{3,0},{4,5},{5,6},{6,7},{7,4},{8,9},{9,10},{10,1... | collective-permute-start | bytes 1572872 | tf_op jit(solution)/shard_map/ppermute | solution.py:22
  252.0 17.5 %collective-permute-start.4 = (bf16[512,512]{1,0:T(8,128)(2,1)}, bf16[512,512]{1,0:T(8,128)(2,1)}, u32[]{:S(2)}, u32[]{:S(2)}) collective-permute-start(bf16[512,512]{1,0:T(8,128)(2,1)} %get-tuple-element.250), channel_id=1, source_target_pairs={{0,3},{1,0},{2,1},{3,2},{4,7},{5,4},{6,5},{7,6},{8,11},{9,8},{10,9... | collective-permute-start | bytes 1572872 | tf_op jit(solution)/shard_map/ppermute | solution.py:25
  263.5 13.5 %collective-permute-start.5 = (bf16[512,512]{1,0:T(8,128)(2,1)}, bf16[512,512]{1,0:T(8,128)(2,1)}, u32[]{:S(2)}, u32[]{:S(2)}) collective-permute-start(bf16[512,512]{1,0:T(8,128)(2,1)} %collective-permute-done.3), channel_id=1, source_target_pairs={{0,1},{1,2},{2,3},{3,0},{4,5},{5,6},{6,7},{7,4},{8,9},{9,10},{10,1... | collective-permute-start | bytes 1572872 | tf_op jit(solution)/shard_map/ppermute | solution.py:22
  267.2 154.5 %reduce-scatter.5.cloned.1.call-start = ((), (), s32[]{:S(2)}) async-start(), calls=%async_computation.3 | async-start | bytes 5242880 | tf_op jit(solution)/shard_map/reduce_scatter | solution.py:61
  267.3 13.9 %copy-start.20 = (f32[2048]{0:T(1024)S(1)}, f32[2048]{0:T(1024)}, u32[]{:S(2)}) copy-start(f32[2048]{0:T(1024)} %param.28) | copy-start | bytes 24580
  267.3 13.9 %copy-start.17 = (bf16[2048,768]{1,0:T(8,128)(2,1)S(1)}, bf16[2048,768]{1,0:T(8,128)(2,1)}, u32[]{:S(2)}) copy-start(bf16[2048,768]{1,0:T(8,128)(2,1)} %param.29) | copy-start | bytes 9437188
  279.0 2.3 copy-start.9
  293.2 79.5 %copy-start.22 = (s32[4]{0:T(128)S(1)}, s32[4]{0:T(128)}, u32[]{:S(2)}) copy-start(s32[4]{0:T(128)} %param.20) | copy-start | bytes 52
Sparse Core Ops, SparseCore 0:
  89.3 53.5 all-gather.4
  199.3 46.2 reduce-scatter.2
  267.4 105.3 all-reduce.1
  375.0 46.6 reduce-scatter.4
